TPU v7x, 512 devices: a whole 4x8x8 slice. The times are simulated.
512 devices in a mesh: group: 8 (over x, y_hi), sub: 64 (over y_lo, z, core).
Axes of the slice: x: 4, y: 8 (y_hi: 2, y_lo: 4; y = y_hi * 4 + y_lo), z: 8, core: 2. Of those that a mesh axis runs over, the one named last changes fastest.
Arguments:
- modes: bfloat16 [524288, 512], P(('group', 'sub')), may hold values from -6 to 6
- block_vals: bfloat16 [24576, 128, 128], P(('group', 'sub')), may hold values from -0.21875 to 0.21875
- block_cols: int32 [24576], P(('group', 'sub')), may hold values from 0 to 7, as said below
- level_maps: bfloat16 [2, 128, 128], replicated, may hold values from -0.5 to 0.5
- psi: bfloat16 [524288, 512], P(('group', 'sub')), may hold values from -0.09375 to 0.09375
- parent_vals: bfloat16 [4096, 128, 128], P(('group', 'sub')), may hold values from -0.09375 to 0.09375
- parent_rows: int32 [4096], P(('group', 'sub')), may hold values from 0 to 63
Outputs:
- parent_coupling: bfloat16 [8192, 1024], P('sub', 'group')
- projected: float32 [4096, 512], P(('group', 'sub'))
Inputs may be any that keep to these rules, and one draw needn't show every extreme that they name: `block_cols`: within one interface row block of one device the 6 vertex blocks are distinct.
All inputs are finite; a program needn't handle non-finite values.
Results may differ from a plain program's by a relative error of at most 0.0078.
Values may be sent and summed in bfloat16 or wider, within the bound.
No kernel may reach another device: no remote copies, remote signals or barrier semaphores. Data moves between devices by JAX's collectives and lax.ppermute only.
A program may use at most 64 MiB of HBM per device.

v0:
```python
import jax
import jax.numpy as jnp
from jax import lax
from jax.sharding import PartitionSpec as P

IFB = 8
BPR = 6


def from_partner(value, axis, mask):
    pairs = [(source, source ^ mask) for source in range(lax.axis_size(axis))]
    return lax.ppermute(value, axis, pairs)


def on_device(modes, block_vals, block_cols, level_maps, psi, parent_vals, parent_rows):
    block_size = block_vals.shape[1]
    width = modes.shape[1]
    vertex_blocks = modes.shape[0] // block_size
    row_blocks = IFB
    levels = min(2, lax.axis_size("group").bit_length() - 1)
    merged = 2**levels
    n_sub = lax.axis_size("sub")
    group_index = lax.axis_index("group")
    vals_all = [parent_vals]
    rows_all = [parent_rows]
    for mask in range(1, merged):
        vals_all.append(from_partner(parent_vals, "group", mask))
        rows_all.append(from_partner(parent_rows, "group", mask))
    vals_all = jnp.concatenate(vals_all, axis=0)
    rows_all = jnp.concatenate(rows_all, axis=0)
    onehot = (
        block_cols.reshape(row_blocks, BPR)[:, :, None] == jnp.arange(vertex_blocks)[None, None, :]
    ).astype(jnp.float32)
    blocks = block_vals.astype(jnp.float32).reshape(row_blocks, BPR, block_size, block_size)
    dense = (
        jnp.einsum("rbc,rbij->ricj", onehot, blocks)
        .reshape(row_blocks * block_size, vertex_blocks * block_size)
        .astype(jnp.bfloat16)
    )
    panel = jnp.dot(dense, modes, preferred_element_type=jnp.float32).astype(jnp.bfloat16)
    for level in range(levels):
        sibling = from_partner(panel, "group", 2**level)
        total = (panel.astype(jnp.float32) + sibling.astype(jnp.float32)).astype(jnp.bfloat16)
        mapped = jnp.einsum(
            "ab,rbm->ram",
            level_maps[level],
            total.reshape(row_blocks, block_size, width),
            preferred_element_type=jnp.float32,
        )
        panel = mapped.reshape(row_blocks * block_size, width).astype(jnp.bfloat16)
    quarter = width // merged
    column = group_index % merged * quarter
    head = lax.dynamic_slice_in_dim(panel[:block_size], column, quarter, 1)
    piece = lax.all_gather(head, "sub", axis=0, tiled=True).reshape(n_sub, block_size, quarter)
    picked = jnp.take(piece, rows_all, axis=0)
    parent_out = jnp.einsum(
        "kab,kbm->am", vals_all, picked, preferred_element_type=jnp.float32
    ).astype(jnp.bfloat16)
    partial = lax.dot_general(
        psi, panel, (((0,), (0,)), ((), ())), preferred_element_type=jnp.float32
    )
    spread = lax.all_to_all(partial.reshape(n_sub, width // n_sub, width), "sub", 0, 0, tiled=True)
    projected = spread.sum(axis=0)
    return (parent_out, projected)


def solution(mesh):
    return jax.shard_map(
        on_device,
        mesh=mesh,
        in_specs=(
            P(("group", "sub"), None),
            P(("group", "sub"), None, None),
            P(("group", "sub")),
            P(),
            P(("group", "sub"), None),
            P(("group", "sub"), None, None),
            P(("group", "sub")),
        ),
        out_specs=(P("sub", "group"), P(("group", "sub"), None)),
        check_vma=False,
    )
```

profile of v0, /device:TPU:1, one launch (start us, length us, event | category | flops | bytes accessed | tf_op | source)
XLA Modules:
  0.0 253.6 jit_solution(811477235119022073)
XLA Ops:
  7.2 0.8 eq.17
  8.1 0.5 copy-done
  8.6 1.0 fusion.5
  9.8 1.2 fusion.8
  11.1 8.4 %collective-permute-start.6 = (bf16[1024,512]{1,0:T(8,128)(2,1)S(1)}, bf16[1024,512]{1,0:T(8,128)(2,1)S(1)}, u32[]{:S(2)}, u32[]{:S(2)}) collective-permute-start(bf16[1024,512]{1,0:T(8,128)(2,1)S(1)} %fusion.8), channel_id=1, source_target_pairs={{0,64},{64,0},{128,192},{192,128},{256,320},{320,256},{384,448},{4... | collective-permute-start | bytes 3145736 | tf_op jit(solution)/shard_map/ppermute | solution.py:12
  19.5 33.9 %collective-permute-done.6 = bf16[1024,512]{1,0:T(8,128)(2,1)S(1)} collective-permute-done((bf16[1024,512]{1,0:T(8,128)(2,1)S(1)}, bf16[1024,512]{1,0:T(8,128)(2,1)S(1)}, u32[]{:S(2)}, u32[]{:S(2)}) %collective-permute-start.6) | collective-permute-done | bytes 1048608 | tf_op jit(solution)/shard_map/ppermute | solution.py:12
  54.2 3.7 %collective-permute-start.7 = (bf16[1024,512]{1,0:T(8,128)(2,1)S(1)}, bf16[1024,512]{1,0:T(8,128)(2,1)}, u32[]{:S(2)}, u32[]{:S(2)}) collective-permute-start(bf16[1024,512]{1,0:T(8,128)(2,1)S(1)} %bitcast.52), channel_id=1, source_target_pairs={{0,128},{64,192},{128,0},{192,64},{256,384},{320,448},{384,256},{4... | collective-permute-start | bytes 3145736 | tf_op jit(solution)/shard_map/ppermute | solution.py:12
  57.9 12.3 %collective-permute-done.7 = bf16[1024,512]{1,0:T(8,128)(2,1)} collective-permute-done((bf16[1024,512]{1,0:T(8,128)(2,1)S(1)}, bf16[1024,512]{1,0:T(8,128)(2,1)}, u32[]{:S(2)}, u32[]{:S(2)}) %collective-permute-start.7) | collective-permute-done | bytes 1048608 | tf_op jit(solution)/shard_map/ppermute | solution.py:12
  70.1 1.5 add_convert_fusion
  72.1 0.6 constant_dynamic-slice_fusion
  72.7 3.0 %convolution_bitcast_fusion = f32[64,8,512]{2,1,0:T(8,128)} fusion(bf16[1024,512]{1,0:T(8,128)(2,1)S(1)} %bitcast.57, bf16[1024,512]{1,0:T(8,128)(2,1)} %param.11), kind=kOutput, calls=%fused_computation.12 | convolution fusion | flops 536870912 | bytes 3145728 | tf_op jit(solution)/shard_map/dot_general | solution.py:59
  75.7 36.6 %all-to-all-start = ((f32[64,8,512]{2,1,0:T(8,128)}), f32[64,8,512]{2,1,0:T(8,128)S(1)}, u32[]{:S(2)}, u32[]{:S(2)}) async-start(f32[64,8,512]{2,1,0:T(8,128)} %convolution_bitcast_fusion), calls=%async_computation | async-start | bytes 2097152 | tf_op jit(solution)/shard_map/all_to_all | solution.py:62
  112.3 4.8 %collective-permute-start.3 = (s32[8]{0:T(128)S(1)}, s32[8]{0:T(128)S(1)}, u32[]{:S(2)}, u32[]{:S(2)}) collective-permute-start(s32[8]{0:T(128)S(1)} %copy-done.2), channel_id=1, source_target_pairs={{0,64},{64,0},{128,192},{192,128},{256,320},{320,256},{384,448},{4... | collective-permute-start | bytes 104 | tf_op jit(solution)/shard_map/ppermute | solution.py:12
  117.2 3.1 %collective-permute-start.4 = (s32[8]{0:T(128)S(1)}, s32[8]{0:T(128)S(1)}, u32[]{:S(2)}, u32[]{:S(2)}) collective-permute-start(s32[8]{0:T(128)S(1)} %copy-done.2), channel_id=1, source_target_pairs={{0,128},{64,192},{128,0},{192,64},{256,384},{320,448},{384,256},{4... | collective-permute-start | bytes 104 | tf_op jit(solution)/shard_map/ppermute | solution.py:12
  120.3 4.3 %collective-permute-start.5 = (s32[8]{0:T(128)S(1)}, s32[8]{0:T(128)S(1)}, u32[]{:S(2)}, u32[]{:S(2)}) collective-permute-start(s32[8]{0:T(128)S(1)} %copy-done.2), channel_id=1, source_target_pairs={{0,192},{64,128},{128,64},{192,0},{256,448},{320,384},{384,320},{4... | collective-permute-start | bytes 104 | tf_op jit(solution)/shard_map/ppermute | solution.py:12
  124.6 4.8 %collective-permute-start = (bf16[8,128,128]{2,1,0:T(8,128)(2,1)S(1)}, bf16[8,128,128]{2,1,0:T(8,128)(2,1)S(1)}, u32[]{:S(2)}, u32[]{:S(2)}) collective-permute-start(bf16[8,128,128]{2,1,0:T(8,128)(2,1)S(1)} %copy-done.4), channel_id=1, source_target_pairs={{0,64},{64,0},{128,192},{192,128},{256,320},{320,256},{384,448},{4... | collective-permute-start | bytes 786440 | tf_op jit(solution)/shard_map/ppermute | solution.py:12
  129.5 3.1 %collective-permute-start.1 = (bf16[8,128,128]{2,1,0:T(8,128)(2,1)S(1)}, bf16[8,128,128]{2,1,0:T(8,128)(2,1)S(1)}, u32[]{:S(2)}, u32[]{:S(2)}) collective-permute-start(bf16[8,128,128]{2,1,0:T(8,128)(2,1)S(1)} %copy-done.4), channel_id=1, source_target_pairs={{0,128},{64,192},{128,0},{192,64},{256,384},{320,448},{384,256},{4... | collective-permute-start | bytes 786440 | tf_op jit(solution)/shard_map/ppermute | solution.py:12
  132.6 0.5 collective-permute-done.3
  133.1 5.8 %collective-permute-start.2 = (bf16[8,128,128]{2,1,0:T(8,128)(2,1)S(1)}, bf16[8,128,128]{2,1,0:T(8,128)(2,1)}, u32[]{:S(2)}, u32[]{:S(2)}) collective-permute-start(bf16[8,128,128]{2,1,0:T(8,128)(2,1)S(1)} %copy-done.4), channel_id=1, source_target_pairs={{0,192},{64,128},{128,64},{192,0},{256,448},{320,384},{384,320},{4... | collective-permute-start | bytes 786440 | tf_op jit(solution)/shard_map/ppermute | solution.py:12
  139.0 25.7 %all-to-all-done = f32[64,8,512]{2,1,0:T(8,128)S(1)} async-done(((f32[64,8,512]{2,1,0:T(8,128)}), f32[64,8,512]{2,1,0:T(8,128)S(1)}, u32[]{:S(2)}, u32[]{:S(2)}) %all-to-all-start) | async-done | bytes 1048608 | tf_op jit(solution)/shard_map/all_to_all | solution.py:62
  164.7 0.7 reduce_sum.9
  165.4 76.8 %all-gather.3.cloned.1.call-done = bf16[1,8192,128]{2,1,0:T(8,128)(2,1)} async-done(((bf16[1,128,128]{2,1,0:T(8,128)(2,1)}), bf16[1,8192,128]{2,1,0:T(8,128)(2,1)}) %all-gather.3.cloned.1.call-update) | async-done | bytes 2097168 | tf_op jit(solution)/shard_map/all_gather | solution.py:54
  242.3 2.3 gather_fusion
  244.7 2.1 fusion.11
  (23 shorter events, 1.6 us)
Async XLA Ops:
  7.2 1.4 copy-start
  7.2 235.1 %all-gather.3.cloned.1.call-start = ((), (), s32[]{:S(2)}) async-start(), calls=%async_computation.1 | async-start | bytes 2129920 | tf_op jit(solution)/shard_map/all_gather | solution.py:54
  8.6 1.2 copy-start.3
  11.1 42.7 %copy-start.1 = (bf16[2,128,128]{2,1,0:T(8,128)(2,1)S(1)}, bf16[2,128,128]{2,1,0:T(8,128)(2,1)}, u32[]{:S(2)}) copy-start(bf16[2,128,128]{2,1,0:T(8,128)(2,1)} %param.10) | copy-start | bytes 196612
  11.1 42.3 %collective-permute-start.6 = (bf16[1024,512]{1,0:T(8,128)(2,1)S(1)}, bf16[1024,512]{1,0:T(8,128)(2,1)S(1)}, u32[]{:S(2)}, u32[]{:S(2)}) collective-permute-start(bf16[1024,512]{1,0:T(8,128)(2,1)S(1)} %fusion.8), channel_id=1, source_target_pairs={{0,64},{64,0},{128,192},{192,128},{256,320},{320,256},{384,448},{4... | collective-permute-start | bytes 3145736 | tf_op jit(solution)/shard_map/ppermute | solution.py:12
  54.2 16.0 %collective-permute-start.7 = (bf16[1024,512]{1,0:T(8,128)(2,1)S(1)}, bf16[1024,512]{1,0:T(8,128)(2,1)}, u32[]{:S(2)}, u32[]{:S(2)}) collective-permute-start(bf16[1024,512]{1,0:T(8,128)(2,1)S(1)} %bitcast.52), channel_id=1, source_target_pairs={{0,128},{64,192},{128,0},{192,64},{256,384},{320,448},{384,256},{4... | collective-permute-start | bytes 3145736 | tf_op jit(solution)/shard_map/ppermute | solution.py:12
  75.7 36.6 %copy-start.2 = (s32[8]{0:T(128)S(1)}, s32[8]{0:T(128)}, u32[]{:S(2)}) copy-start(s32[8]{0:T(128)} %param.13) | copy-start | bytes 100
  75.7 48.9 %copy-start.4 = (bf16[8,128,128]{2,1,0:T(8,128)(2,1)S(1)}, bf16[8,128,128]{2,1,0:T(8,128)(2,1)}, u32[]{:S(2)}) copy-start(bf16[8,128,128]{2,1,0:T(8,128)(2,1)} %param.12) | copy-start | bytes 786436
  75.7 89.0 %all-to-all-start = ((f32[64,8,512]{2,1,0:T(8,128)}), f32[64,8,512]{2,1,0:T(8,128)S(1)}, u32[]{:S(2)}, u32[]{:S(2)}) async-start(f32[64,8,512]{2,1,0:T(8,128)} %convolution_bitcast_fusion), calls=%async_computation | async-start | bytes 2097152 | tf_op jit(solution)/shard_map/all_to_all | solution.py:62
  112.3 20.8 %collective-permute-start.3 = (s32[8]{0:T(128)S(1)}, s32[8]{0:T(128)S(1)}, u32[]{:S(2)}, u32[]{:S(2)}) collective-permute-start(s32[8]{0:T(128)S(1)} %copy-done.2), channel_id=1, source_target_pairs={{0,64},{64,0},{128,192},{192,128},{256,320},{320,256},{384,448},{4... | collective-permute-start | bytes 104 | tf_op jit(solution)/shard_map/ppermute | solution.py:12
  117.2 21.7 %collective-permute-start.4 = (s32[8]{0:T(128)S(1)}, s32[8]{0:T(128)S(1)}, u32[]{:S(2)}, u32[]{:S(2)}) collective-permute-start(s32[8]{0:T(128)S(1)} %copy-done.2), channel_id=1, source_target_pairs={{0,128},{64,192},{128,0},{192,64},{256,384},{320,448},{384,256},{4... | collective-permute-start | bytes 104 | tf_op jit(solution)/shard_map/ppermute | solution.py:12
  120.3 18.6 %collective-permute-start.5 = (s32[8]{0:T(128)S(1)}, s32[8]{0:T(128)S(1)}, u32[]{:S(2)}, u32[]{:S(2)}) collective-permute-start(s32[8]{0:T(128)S(1)} %copy-done.2), channel_id=1, source_target_pairs={{0,192},{64,128},{128,64},{192,0},{256,448},{320,384},{384,320},{4... | collective-permute-start | bytes 104 | tf_op jit(solution)/shard_map/ppermute | solution.py:12
  124.6 120.0 %collective-permute-start = (bf16[8,128,128]{2,1,0:T(8,128)(2,1)S(1)}, bf16[8,128,128]{2,1,0:T(8,128)(2,1)S(1)}, u32[]{:S(2)}, u32[]{:S(2)}) collective-permute-start(bf16[8,128,128]{2,1,0:T(8,128)(2,1)S(1)} %copy-done.4), channel_id=1, source_target_pairs={{0,64},{64,0},{128,192},{192,128},{256,320},{320,256},{384,448},{4... | collective-permute-start | bytes 786440 | tf_op jit(solution)/shard_map/ppermute | solution.py:12
  129.5 115.2 %collective-permute-start.1 = (bf16[8,128,128]{2,1,0:T(8,128)(2,1)S(1)}, bf16[8,128,128]{2,1,0:T(8,128)(2,1)S(1)}, u32[]{:S(2)}, u32[]{:S(2)}) collective-permute-start(bf16[8,128,128]{2,1,0:T(8,128)(2,1)S(1)} %copy-done.4), channel_id=1, source_target_pairs={{0,128},{64,192},{128,0},{192,64},{256,384},{320,448},{384,256},{4... | collective-permute-start | bytes 786440 | tf_op jit(solution)/shard_map/ppermute | solution.py:12
  133.1 111.6 %collective-permute-start.2 = (bf16[8,128,128]{2,1,0:T(8,128)(2,1)S(1)}, bf16[8,128,128]{2,1,0:T(8,128)(2,1)}, u32[]{:S(2)}, u32[]{:S(2)}) collective-permute-start(bf16[8,128,128]{2,1,0:T(8,128)(2,1)S(1)} %copy-done.4), channel_id=1, source_target_pairs={{0,192},{64,128},{128,64},{192,0},{256,448},{320,384},{384,320},{4... | collective-permute-start | bytes 786440 | tf_op jit(solution)/shard_map/ppermute | solution.py:12
Sparse Core Ops, SparseCore 0:
  72.9 169.3 all-gather.2
where the time goes:
time: 254 us
  waiting for transfers between devices  149 us (59%)
  starting transfers between devices  74.7 us (29%)
  between operations  14.3 us (6%)
  matrix products  8.17 us (3%)
  local copies, waits for them, and re-layouts  4.54 us (2%)
  other arithmetic  2.7 us (1%)
    all_gather x1, waiting for transfers between devices, on_device(): lax.all_gather(head, 'sub', axis=0, tiled=True)  76.8 us
    ppermute x8, waiting for transfers between devices, from_partner(): return lax.ppermute(value, axis, pairs)  46.7 us
    ppermute x8, starting transfers between devices, from_partner(): return lax.ppermute(value, axis, pairs)  38.1 us
    all_to_all x1, starting transfers between devices, on_device(): lax.all_to_all(partial.reshape(n_sub, width // n_sub, width), 'sub', 0, 0...  36.6 us
    all_to_all x1, waiting for transfers between devices, on_device(): lax.all_to_all(partial.reshape(n_sub, width // n_sub, width), 'sub', 0, 0...  25.7 us
  transfers between devices with their start and end apart: 10, of which 5 were waited for; matrix products, arithmetic and copies ran while one was open for 2% of the time, Pallas kernels for 0%

commit v1 on v0

--- a/solution.py
+++ b/solution.py
@@ -51,7 +51,14 @@
     quarter = width // merged
     column = group_index % merged * quarter
     head = lax.dynamic_slice_in_dim(panel[:block_size], column, quarter, 1)
-    piece = lax.all_gather(head, "sub", axis=0, tiled=True).reshape(n_sub, block_size, quarter)
+
+    def draft_the_quarters(w_in):
+        history = []
+        for _ in range(lax.axis_size("sub")):
+            history.append(w_in)
+        return jnp.concatenate(lax.all_to_all(jnp.stack(history, axis=0), "sub", 0, 0), axis=0)
+
+    piece = draft_the_quarters(head).reshape(n_sub, block_size, quarter)
     picked = jnp.take(piece, rows_all, axis=0)
     parent_out = jnp.einsum(
         "kab,kbm->am", vals_all, picked, preferred_element_type=jnp.float32

time: 254 us -> 218 us (0.86)
  waiting for transfers between devices: 149 us -> 121 us
  between operations: 14.3 us -> 0.89 us
  starting transfers between devices: 74.7 us -> 79.6 us
    all_gather x1 -> x0, waiting for transfers between devices: 76.8 us -> none  [on_device(): lax.all_gather(head, 'sub', axis=0, tiled=True)]
    ppermute x8, waiting for transfers between devices: 46.7 us -> 77.4 us  [from_partner(): return lax.ppermute(value, axis, pairs)]
    all_to_all x0 -> x1, waiting for transfers between devices: none -> 15.5 us  [draft_the_quarters(): lax.all_to_all(jnp.stack(history, axis=0), 'sub', 0, 0)]
    all_to_all x0 -> x1, starting transfers between devices: none -> 6.18 us  [draft_the_quarters(): lax.all_to_all(jnp.stack(history, axis=0), 'sub', 0, 0)]
where the time goes in v1:
time: 218 us; the launch traced here: 216 us
  waiting for transfers between devices  121 us (56%)
  starting transfers between devices  79.6 us (37%)
  matrix products  6.97 us (3%)
  local copies, waits for them, and re-layouts  6.73 us (3%)
    ppermute x8, waiting for transfers between devices, from_partner(): return lax.ppermute(value, axis, pairs)  77.4 us
    ppermute x8, starting transfers between devices, from_partner(): return lax.ppermute(value, axis, pairs)  37 us
    all_to_all x1, starting transfers between devices, on_device(): lax.all_to_all(partial.reshape(n_sub, width // n_sub, width), 'sub', 0, 0...  36.5 us
    all_to_all x1, waiting for transfers between devices, on_device(): lax.all_to_all(partial.reshape(n_sub, width // n_sub, width), 'sub', 0, 0...  27.7 us
    all_to_all x1, waiting for transfers between devices, draft_the_quarters(): lax.all_to_all(jnp.stack(history, axis=0), 'sub', 0, 0)  15.5 us
    all_to_all x1, starting transfers between devices, draft_the_quarters(): lax.all_to_all(jnp.stack(history, axis=0), 'sub', 0, 0)  6.18 us
  transfers between devices with their start and end apart: 10, of which 5 were waited for; matrix products, arithmetic and copies ran while one was open for 2% of the time, Pallas kernels for 0%

profile of v1, /device:TPU:1, one launch (start us, length us, event | category | flops | bytes accessed | tf_op | source)
XLA Modules:
  0.0 216.4 jit_solution(8641482025308574498)
XLA Ops:
  0.6 0.8 eq.17
  2.1 1.0 fusion.5
  3.3 1.2 fusion.8
  4.5 8.4 %collective-permute-start.6 = (bf16[1024,512]{1,0:T(8,128)(2,1)S(1)}, bf16[1024,512]{1,0:T(8,128)(2,1)S(1)}, u32[]{:S(2)}, u32[]{:S(2)}) collective-permute-start(bf16[1024,512]{1,0:T(8,128)(2,1)S(1)} %fusion.8), channel_id=1, source_target_pairs={{0,64},{64,0},{128,192},{192,128},{256,320},{320,256},{384,448},{4... | collective-permute-start | bytes 3145736 | tf_op jit(solution)/shard_map/ppermute | solution.py:12
  13.0 33.9 %collective-permute-done.6 = bf16[1024,512]{1,0:T(8,128)(2,1)S(1)} collective-permute-done((bf16[1024,512]{1,0:T(8,128)(2,1)S(1)}, bf16[1024,512]{1,0:T(8,128)(2,1)S(1)}, u32[]{:S(2)}, u32[]{:S(2)}) %collective-permute-start.6) | collective-permute-done | bytes 1048608 | tf_op jit(solution)/shard_map/ppermute | solution.py:12
  47.6 3.8 %collective-permute-start.7 = (bf16[1024,512]{1,0:T(8,128)(2,1)S(1)}, bf16[1024,512]{1,0:T(8,128)(2,1)S(1)}, u32[]{:S(2)}, u32[]{:S(2)}) collective-permute-start(bf16[1024,512]{1,0:T(8,128)(2,1)S(1)} %bitcast.53), channel_id=1, source_target_pairs={{0,128},{64,192},{128,0},{192,64},{256,384},{320,448},{384,256},{4... | collective-permute-start | bytes 3145736 | tf_op jit(solution)/shard_map/ppermute | solution.py:12
  51.4 12.2 %collective-permute-done.7 = bf16[1024,512]{1,0:T(8,128)(2,1)S(1)} collective-permute-done((bf16[1024,512]{1,0:T(8,128)(2,1)S(1)}, bf16[1024,512]{1,0:T(8,128)(2,1)S(1)}, u32[]{:S(2)}, u32[]{:S(2)}) %collective-permute-start.7) | collective-permute-done | bytes 1048608 | tf_op jit(solution)/shard_map/ppermute | solution.py:12
  64.4 1.8 convolution_bitcast_fusion
  66.2 36.5 %all-to-all-start.1 = ((f32[64,8,512]{2,1,0:T(8,128)}), f32[64,8,512]{2,1,0:T(8,128)S(1)}, u32[]{:S(2)}, u32[]{:S(2)}) async-start(f32[64,8,512]{2,1,0:T(8,128)} %convolution_bitcast_fusion), calls=%async_computation.1 | async-start | bytes 2097152 | tf_op jit(solution)/shard_map/all_to_all | solution.py:69
  102.7 0.9 slice.15
  103.6 27.7 %all-to-all-done.1 = f32[64,8,512]{2,1,0:T(8,128)S(1)} async-done(((f32[64,8,512]{2,1,0:T(8,128)}), f32[64,8,512]{2,1,0:T(8,128)S(1)}, u32[]{:S(2)}, u32[]{:S(2)}) %all-to-all-start.1) | async-done | bytes 1048608 | tf_op jit(solution)/shard_map/all_to_all | solution.py:69
  131.3 1.8 stack.2
  133.1 6.2 %all-to-all-start = ((bf16[64,128,128]{2,1,0:T(8,128)(2,1)}), bf16[64,128,128]{2,1,0:T(8,128)(2,1)}, u32[]{:S(2)}, u32[]{:S(2)}) async-start(bf16[64,128,128]{2,1,0:T(8,128)(2,1)} %stack.2), calls=%async_computation | async-start | bytes 4194304 | tf_op jit(solution)/shard_map/all_to_all | solution.py:59
  139.3 6.0 %collective-permute-start.5 = (s32[8]{0:T(128)S(1)}, s32[8]{0:T(128)S(1)}, u32[]{:S(2)}, u32[]{:S(2)}) collective-permute-start(s32[8]{0:T(128)S(1)} %copy-done.3), channel_id=1, source_target_pairs={{0,192},{64,128},{128,64},{192,0},{256,448},{320,384},{384,320},{4... | collective-permute-start | bytes 104 | tf_op jit(solution)/shard_map/ppermute | solution.py:12
  145.3 2.1 collective-permute-start.4
  147.5 4.1 %collective-permute-start.3 = (s32[8]{0:T(128)S(1)}, s32[8]{0:T(128)S(1)}, u32[]{:S(2)}, u32[]{:S(2)}) collective-permute-start(s32[8]{0:T(128)S(1)} %copy-done.3), channel_id=1, source_target_pairs={{0,64},{64,0},{128,192},{192,128},{256,320},{320,256},{384,448},{4... | collective-permute-start | bytes 104 | tf_op jit(solution)/shard_map/ppermute | solution.py:12
  151.6 3.1 %collective-permute-start.1 = (bf16[8,128,128]{2,1,0:T(8,128)(2,1)S(1)}, bf16[8,128,128]{2,1,0:T(8,128)(2,1)S(1)}, u32[]{:S(2)}, u32[]{:S(2)}) collective-permute-start(bf16[8,128,128]{2,1,0:T(8,128)(2,1)S(1)} %copy-done.6), channel_id=1, source_target_pairs={{0,128},{64,192},{128,0},{192,64},{256,384},{320,448},{384,256},{4... | collective-permute-start | bytes 786440 | tf_op jit(solution)/shard_map/ppermute | solution.py:12
  154.8 5.1 %collective-permute-start = (bf16[8,128,128]{2,1,0:T(8,128)(2,1)S(1)}, bf16[8,128,128]{2,1,0:T(8,128)(2,1)S(1)}, u32[]{:S(2)}, u32[]{:S(2)}) collective-permute-start(bf16[8,128,128]{2,1,0:T(8,128)(2,1)S(1)} %copy-done.6), channel_id=1, source_target_pairs={{0,64},{64,0},{128,192},{192,128},{256,320},{320,256},{384,448},{4... | collective-permute-start | bytes 786440 | tf_op jit(solution)/shard_map/ppermute | solution.py:12
  159.8 31.3 %collective-permute-done.5 = s32[8]{0:T(128)S(1)} collective-permute-done((s32[8]{0:T(128)S(1)}, s32[8]{0:T(128)S(1)}, u32[]{:S(2)}, u32[]{:S(2)}) %collective-permute-start.5) | collective-permute-done | bytes 64 | tf_op jit(solution)/shard_map/ppermute | solution.py:12
  191.2 4.3 %collective-permute-start.2 = (bf16[8,128,128]{2,1,0:T(8,128)(2,1)S(1)}, bf16[8,128,128]{2,1,0:T(8,128)(2,1)}, u32[]{:S(2)}, u32[]{:S(2)}) collective-permute-start(bf16[8,128,128]{2,1,0:T(8,128)(2,1)S(1)} %copy-done.6), channel_id=1, source_target_pairs={{0,192},{64,128},{128,64},{192,0},{256,448},{320,384},{384,320},{4... | collective-permute-start | bytes 786440 | tf_op jit(solution)/shard_map/ppermute | solution.py:12
  195.7 0.7 reduce_sum.9
  196.4 15.5 %all-to-all-done = bf16[64,128,128]{2,1,0:T(8,128)(2,1)} async-done(((bf16[64,128,128]{2,1,0:T(8,128)(2,1)}), bf16[64,128,128]{2,1,0:T(8,128)(2,1)}, u32[]{:S(2)}, u32[]{:S(2)}) %all-to-all-start) | async-done | bytes 2097184 | tf_op jit(solution)/shard_map/all_to_all | solution.py:59
  211.9 2.3 %gather_fusion = bf16[32,128,128]{2,1,0:T(8,128)(2,1)S(1)} fusion(bf16[64,128,128]{2,1,0:T(8,128)(2,1)} %all-to-all-done, s32[1024]{0:T(1024)S(1)} %pad_clamp_fusion), kind=kCustom, calls=%fused_computation | custom fusion | bytes 2097280 | tf_op jit(solution)/shard_map/jit(_take)/gather | solution.py:62
  214.3 2.1 fusion.11
  (27 shorter events, 2.5 us)
Async XLA Ops:
  0.6 1.4 copy-start
  2.1 1.2 copy-start.4
  4.5 42.6 %copy-start.2 = (bf16[2,128,128]{2,1,0:T(8,128)(2,1)S(1)}, bf16[2,128,128]{2,1,0:T(8,128)(2,1)}, u32[]{:S(2)}) copy-start(bf16[2,128,128]{2,1,0:T(8,128)(2,1)} %param.10) | copy-start | bytes 196612
  4.5 42.3 %collective-permute-start.6 = (bf16[1024,512]{1,0:T(8,128)(2,1)S(1)}, bf16[1024,512]{1,0:T(8,128)(2,1)S(1)}, u32[]{:S(2)}, u32[]{:S(2)}) collective-permute-start(bf16[1024,512]{1,0:T(8,128)(2,1)S(1)} %fusion.8), channel_id=1, source_target_pairs={{0,64},{64,0},{128,192},{192,128},{256,320},{320,256},{384,448},{4... | collective-permute-start | bytes 3145736 | tf_op jit(solution)/shard_map/ppermute | solution.py:12
  47.6 16.8 %copy-start.5 = (bf16[1024,512]{1,0:T(8,128)(2,1)S(1)}, bf16[1024,512]{1,0:T(8,128)(2,1)}, u32[]{:S(2)}) copy-start(bf16[1024,512]{1,0:T(8,128)(2,1)} %param.11) | copy-start | bytes 3145732
  47.6 16.0 %collective-permute-start.7 = (bf16[1024,512]{1,0:T(8,128)(2,1)S(1)}, bf16[1024,512]{1,0:T(8,128)(2,1)S(1)}, u32[]{:S(2)}, u32[]{:S(2)}) collective-permute-start(bf16[1024,512]{1,0:T(8,128)(2,1)S(1)} %bitcast.53), channel_id=1, source_target_pairs={{0,128},{64,192},{128,0},{192,64},{256,384},{320,448},{384,256},{4... | collective-permute-start | bytes 3145736 | tf_op jit(solution)/shard_map/ppermute | solution.py:12
  64.4 1.8 copy-start.1
  66.2 65.1 %all-to-all-start.1 = ((f32[64,8,512]{2,1,0:T(8,128)}), f32[64,8,512]{2,1,0:T(8,128)S(1)}, u32[]{:S(2)}, u32[]{:S(2)}) async-start(f32[64,8,512]{2,1,0:T(8,128)} %convolution_bitcast_fusion), calls=%async_computation.1 | async-start | bytes 2097152 | tf_op jit(solution)/shard_map/all_to_all | solution.py:69
  133.1 6.2 %copy-start.3 = (s32[8]{0:T(128)S(1)}, s32[8]{0:T(128)}, u32[]{:S(2)}) copy-start(s32[8]{0:T(128)} %param.13) | copy-start | bytes 100
  133.1 18.5 %copy-start.6 = (bf16[8,128,128]{2,1,0:T(8,128)(2,1)S(1)}, bf16[8,128,128]{2,1,0:T(8,128)(2,1)}, u32[]{:S(2)}) copy-start(bf16[8,128,128]{2,1,0:T(8,128)(2,1)} %param.12) | copy-start | bytes 786436
  133.1 78.8 %all-to-all-start = ((bf16[64,128,128]{2,1,0:T(8,128)(2,1)}), bf16[64,128,128]{2,1,0:T(8,128)(2,1)}, u32[]{:S(2)}, u32[]{:S(2)}) async-start(bf16[64,128,128]{2,1,0:T(8,128)(2,1)} %stack.2), calls=%async_computation | async-start | bytes 4194304 | tf_op jit(solution)/shard_map/all_to_all | solution.py:59
  139.3 51.8 %collective-permute-start.5 = (s32[8]{0:T(128)S(1)}, s32[8]{0:T(128)S(1)}, u32[]{:S(2)}, u32[]{:S(2)}) collective-permute-start(s32[8]{0:T(128)S(1)} %copy-done.3), channel_id=1, source_target_pairs={{0,192},{64,128},{128,64},{192,0},{256,448},{320,384},{384,320},{4... | collective-permute-start | bytes 104 | tf_op jit(solution)/shard_map/ppermute | solution.py:12
  145.3 50.2 %collective-permute-start.4 = (s32[8]{0:T(128)S(1)}, s32[8]{0:T(128)S(1)}, u32[]{:S(2)}, u32[]{:S(2)}) collective-permute-start(s32[8]{0:T(128)S(1)} %copy-done.3), channel_id=1, source_target_pairs={{0,128},{64,192},{128,0},{192,64},{256,384},{320,448},{384,256},{4... | collective-permute-start | bytes 104 | tf_op jit(solution)/shard_map/ppermute | solution.py:12
  147.5 48.1 %collective-permute-start.3 = (s32[8]{0:T(128)S(1)}, s32[8]{0:T(128)S(1)}, u32[]{:S(2)}, u32[]{:S(2)}) collective-permute-start(s32[8]{0:T(128)S(1)} %copy-done.3), channel_id=1, source_target_pairs={{0,64},{64,0},{128,192},{192,128},{256,320},{320,256},{384,448},{4... | collective-permute-start | bytes 104 | tf_op jit(solution)/shard_map/ppermute | solution.py:12
  151.6 62.7 %collective-permute-start.1 = (bf16[8,128,128]{2,1,0:T(8,128)(2,1)S(1)}, bf16[8,128,128]{2,1,0:T(8,128)(2,1)S(1)}, u32[]{:S(2)}, u32[]{:S(2)}) collective-permute-start(bf16[8,128,128]{2,1,0:T(8,128)(2,1)S(1)} %copy-done.6), channel_id=1, source_target_pairs={{0,128},{64,192},{128,0},{192,64},{256,384},{320,448},{384,256},{4... | collective-permute-start | bytes 786440 | tf_op jit(solution)/shard_map/ppermute | solution.py:12
  154.8 59.5 %collective-permute-start = (bf16[8,128,128]{2,1,0:T(8,128)(2,1)S(1)}, bf16[8,128,128]{2,1,0:T(8,128)(2,1)S(1)}, u32[]{:S(2)}, u32[]{:S(2)}) collective-permute-start(bf16[8,128,128]{2,1,0:T(8,128)(2,1)S(1)} %copy-done.6), channel_id=1, source_target_pairs={{0,64},{64,0},{128,192},{192,128},{256,320},{320,256},{384,448},{4... | collective-permute-start | bytes 786440 | tf_op jit(solution)/shard_map/ppermute | solution.py:12
  191.2 23.1 %collective-permute-start.2 = (bf16[8,128,128]{2,1,0:T(8,128)(2,1)S(1)}, bf16[8,128,128]{2,1,0:T(8,128)(2,1)}, u32[]{:S(2)}, u32[]{:S(2)}) collective-permute-start(bf16[8,128,128]{2,1,0:T(8,128)(2,1)S(1)} %copy-done.6), channel_id=1, source_target_pairs={{0,192},{64,128},{128,64},{192,0},{256,448},{320,384},{384,320},{4... | collective-permute-start | bytes 786440 | tf_op jit(solution)/shard_map/ppermute | solution.py:12
